TPU v7x, 256 devices: a whole 4x4x8 slice. The times are simulated.
256 devices in a mesh: sample: 32 (over z, y_hi, core), tensor: 8 (over y_lo, x).
Axes of the slice: x: 4, y: 4 (y_hi: 2, y_lo: 2; y = y_hi * 2 + y_lo), z: 8, core: 2. Of those that a mesh axis runs over, the one named last changes fastest.
Arguments:
- hidden: bfloat16 [8192, 14336], P('sample', 'tensor'), may hold values from -6 to 6
- down_weight: bfloat16 [4096, 14336], P('sample', 'tensor'), may hold values from -0.046875 to 0.046875
- cotangent: bfloat16 [8192, 4096], P('sample'), may hold values from -6 to 6
- scores: int32 [128], P('sample'), may hold values from 0 to 38654
- prompt_ids: int32 [128], P('sample'), may hold values from 0 to 3, as said below
Outputs:
- layer_out: bfloat16 [8192, 4096], P('sample', 'tensor')
- hidden_grad: bfloat16 [8192, 14336], P('sample', 'tensor')
- weight_grad: bfloat16 [4096, 14336], P('sample', 'tensor')
Inputs may be any that keep to these rules, and one draw needn't show every extreme that they name: `prompt_ids`: each prompt id names exactly 32 responses.
All inputs are finite; a program needn't handle non-finite values.
Results may differ from a plain program's by a relative error of at most 0.015.
Values may be sent and summed in bfloat16 or wider, within the bound.
No kernel may reach another device: no remote copies, remote signals or barrier semaphores. Data moves between devices by JAX's collectives and lax.ppermute only.
A program may use at most 128 MiB of HBM per device.

v0:
```python
import math
import jax
import jax.numpy as jnp
from jax import lax
from jax.sharding import Mesh
from jax.sharding import PartitionSpec as P

GROUP = 32
SAMPLE = ("z", "yhi", "core")


def sum_to_bf16(received, axis):
    return jnp.sum(received.astype(jnp.float32), axis=axis).astype(jnp.bfloat16)


def shards(hidden, down_weight, cotangent, scores, prompt_ids):
    samples_here = scores.shape[0]
    n_sample = lax.axis_size(SAMPLE)
    n_z = lax.axis_size("z")
    n_yhi = lax.axis_size("yhi")
    n_core = lax.axis_size("core")
    n_tensor = lax.axis_size("tensor")
    prompts = samples_here * n_sample // GROUP
    packed = jnp.concatenate([scores, prompt_ids])[None, :]
    everything = lax.all_gather(packed, SAMPLE, axis=0, tiled=True)
    all_scores = everything[:, :samples_here].reshape(-1)
    all_ids = everything[:, samples_here:].reshape(-1)
    all_rewards = all_scores.astype(jnp.float32) / 64.0
    all_onehot = all_ids[:, None] == jnp.arange(prompts, dtype=jnp.int32)[None, :]
    peak = jnp.max(jnp.where(all_onehot, all_rewards[:, None], jnp.float32(-1e30)), axis=0)
    shifted = jnp.where(all_onehot, jnp.exp(all_rewards[:, None] - peak[None, :]), 0.0)
    total = jnp.sum(shifted, axis=0)
    log_norm = peak + jnp.log(total)
    rewards = scores.astype(jnp.float32) / 64.0
    onehot = prompt_ids[:, None] == jnp.arange(prompts, dtype=jnp.int32)[None, :]
    sample_norm = jnp.sum(jnp.where(onehot, log_norm[None, :], 0.0), axis=1)
    tokens_here = hidden.shape[0]
    token_weight = jnp.repeat(GROUP * jnp.exp(rewards - sample_norm), tokens_here // samples_here)
    weighted = (cotangent.astype(jnp.float32) * token_weight[:, None]).astype(jnp.bfloat16)
    rows_w = down_weight.shape[0]
    d_all = weighted.shape[1]
    d_half = d_all // n_core
    own_first = lax.axis_index("yhi") == 0
    my_core = lax.axis_index("core")
    swap = [(0, 1), (1, 0)]
    weighted_5 = weighted.reshape(tokens_here, n_z, n_yhi, n_core, rows_w)
    weighted_rel = jnp.where(own_first, weighted_5, jnp.flip(weighted_5, axis=2))
    weighted_mine = lax.dynamic_index_in_dim(weighted_rel, my_core, axis=3, keepdims=False)
    weighted_mine = weighted_mine.reshape(tokens_here, d_half)
    weighted_theirs = lax.dynamic_index_in_dim(weighted_rel, 1 - my_core, axis=3, keepdims=False)
    weighted_recv = lax.ppermute(weighted_theirs.reshape(tokens_here, d_half), "core", swap)
    hidden_recv = lax.ppermute(hidden, "core", swap)
    gathered = jnp.concatenate([down_weight, lax.ppermute(down_weight, "yhi", swap)], axis=0)
    gathered = lax.all_gather(gathered, "z", axis=0, tiled=True)
    scale = 1.0 / math.sqrt(tokens_here * n_sample)
    grad_part = (
        lax.dot_general(
            jnp.concatenate([weighted_mine, weighted_recv], axis=0),
            jnp.concatenate([hidden, hidden_recv], axis=0),
            (((0,), (0,)), ((), ())),
            preferred_element_type=jnp.float32,
        )
        * scale
    ).astype(jnp.bfloat16)
    grad_part = lax.psum_scatter(grad_part, "z", scatter_dimension=0, tiled=True)
    weight_grad = (
        grad_part[:rows_w].astype(jnp.float32)
        + lax.ppermute(grad_part[rows_w:], "yhi", swap).astype(jnp.float32)
    ).astype(jnp.bfloat16)

    def value_of(rows):
        return lax.dot_general(
            rows, gathered, (((1,), (1,)), ((), ())), preferred_element_type=jnp.float32
        ).astype(jnp.bfloat16)

    value_mine = value_of(hidden)
    value_recv = lax.ppermute(value_of(hidden_recv), "core", swap)
    partial_value = jnp.stack([value_mine, value_recv], axis=1)
    partial_value = jnp.where(my_core == 0, partial_value, jnp.flip(partial_value, axis=1))
    partial_value = partial_value.reshape(tokens_here, n_core, n_z, n_yhi, rows_w).transpose(
        0, 2, 3, 1, 4
    )
    partial_value = jnp.where(own_first, partial_value, jnp.flip(partial_value, axis=2)).reshape(
        tokens_here, n_tensor, d_all // n_tensor
    )
    layer_out = sum_to_bf16(lax.all_to_all(partial_value, "tensor", 1, 1, tiled=True), 1)
    grad_for_other = jnp.dot(weighted_recv, gathered, preferred_element_type=jnp.float32)
    hidden_grad = (
        jnp.dot(weighted_mine, gathered, preferred_element_type=jnp.float32)
        + lax.ppermute(grad_for_other, "core", swap)
    ).astype(jnp.bfloat16)
    return (layer_out, hidden_grad, weight_grad)


def solution(mesh):
    n_tensor = mesh.shape["tensor"]
    fine = Mesh(mesh.devices.reshape(-1, 2, 2, n_tensor), ("z", "yhi", "core", "tensor"))
    return jax.shard_map(
        shards,
        mesh=fine,
        in_specs=(P(SAMPLE, "tensor"), P(SAMPLE, "tensor"), P(SAMPLE, None), P(SAMPLE), P(SAMPLE)),
        out_specs=(P(SAMPLE, "tensor"), P(SAMPLE, "tensor"), P(SAMPLE, "tensor")),
        check_vma=False,
    )
```

profile of v0, /device:TPU:2, one launch (start us, length us, event | category | flops | bytes accessed | tf_op | source)
XLA Modules:
  0.0 221.6 jit_solution(11949393025093331972)
XLA Ops:
  7.3 3.3 %collective-permute-start = (bf16[128,1792]{1,0:T(8,128)(2,1)}, bf16[128,1792]{1,0:T(8,128)(2,1)S(1)}, u32[]{:S(2)}, u32[]{:S(2)}) collective-permute-start(bf16[128,1792]{1,0:T(8,128)(2,1)} %param.6), channel_id=1, source_target_pairs={{0,16},{16,0},{1,17},{17,1},{2,18},{18,2},{3,19},{19,3},{4,20},{20... | collective-permute-start | bytes 1376264 | tf_op jit(solution)/shard_map/ppermute | solution.py:53
  10.5 10.8 %collective-permute-done = bf16[128,1792]{1,0:T(8,128)(2,1)S(1)} collective-permute-done((bf16[128,1792]{1,0:T(8,128)(2,1)}, bf16[128,1792]{1,0:T(8,128)(2,1)S(1)}, u32[]{:S(2)}, u32[]{:S(2)}) %collective-permute-start) | collective-permute-done | bytes 458784 | tf_op jit(solution)/shard_map/ppermute | solution.py:53
  21.3 2.0 pad_maximum_fusion.1
  23.4 0.6 dynamic-slice
  24.8 21.3 %all-reduce = s32[256]{0:T(256)S(1)} all-reduce(s32[256]{0:T(256)S(1)} %add_dynamic-update-slice_fusion), channel_id=2, replica_groups=mesh['z'=8,'yhi'=2,'core'=2,'tensor'=8] {'z','yhi','core'}, use_global_device_ids=true, to_apply=%add | all-reduce | flops 256 | bytes 2048
  47.2 2.5 %copy.26 = bf16[256,4096]{0,1:T(8,128)(2,1)} copy(bf16[256,4096]{1,0:T(8,128)(2,1)S(1)} %copy-done.1) | data formatting | bytes 4194304 | tf_op args[2]
  49.8 2.0 multiply_convert_fusion.1
  51.8 3.2 %copy.28 = bf16[256,8,2,2,128]{4,1,3,2,0:T(8,128)(2,1)} copy(bf16[256,8,2,2,128]{0,4,3,2,1:T(8,128)(2,1)S(1)} %bitcast.22) | data formatting | bytes 4194304 | tf_op jit(solution)/shard_map/reshape | solution.py:46
  55.0 2.8 %reverse_select_fusion = bf16[256,8,2,2,128]{4,1,3,2,0:T(8,128)(2,1)S(1)} fusion(bf16[256,8,2,2,128]{4,1,3,2,0:T(8,128)(2,1)} %copy.28, pred[]{:T(512)S(6)} %eq.34), kind=kLoop, calls=%fused_computation.2 | loop fusion | flops 1048576 | bytes 4194305 | tf_op jit(solution)/shard_map/jit(_where)/select_n | solution.py:47
  57.8 0.4 constant_dynamic-slice_fusion.1
  58.2 1.6 copy.30
  59.7 0.5 collective-permute-start.1
  60.3 0.8 copy.29
  61.0 3.0 %collective-permute-done.1 = bf16[256,1792]{1,0:T(8,128)(2,1)} collective-permute-done((bf16[256,1792]{1,0:T(8,128)(2,1)}, bf16[256,1792]{1,0:T(8,128)(2,1)}, u32[]{:S(2)}, u32[]{:S(2)}) %collective-permute-start.1) | collective-permute-done | bytes 917536 | tf_op jit(solution)/shard_map/ppermute | solution.py:52
  64.1 7.5 %multiply_convert_fusion = bf16[2048,1792]{1,0:T(8,128)(2,1)} fusion(bf16[256,2048]{0,1:T(8,128)(2,1)S(1)} %collective-permute-done.3, bf16[256,2048]{0,1:T(8,128)(2,1)S(1)} %bitcast.26, bf16[256,1792]{1,0:T(8,128)(2,1)} %collective-permute-done.1, bf16[256,1792]{1,0:T(8,128)(2,1)} %param.5), kind=kOutput, calls=%fused_computation | convolution fusion | flops 3773300736 | bytes 11272192 | tf_op jit(solution)/shard_map/dot_general | solution.py:57
  71.6 39.2 %all-gather.3.cloned.1.call-done = bf16[2048,1792]{1,0:T(8,128)(2,1)} async-done(((bf16[256,1792]{1,0:T(8,128)(2,1)}), bf16[2048,1792]{1,0:T(8,128)(2,1)}) %all-gather.3.cloned.1.call-update) | async-done | bytes 7340048 | tf_op jit(solution)/shard_map/all_gather | solution.py:54
  110.9 5.5 %fusion.2 = bf16[256,2048]{0,1:T(8,128)(2,1)S(1)} fusion(bf16[2048,1792]{1,0:T(8,128)(2,1)} %all-gather.3.cloned.1.call-done, bf16[256,1792]{1,0:T(8,128)(2,1)} %collective-permute-done.1), kind=kOutput, calls=%fused_computation.10 | convolution fusion | flops 1879572480 | bytes 9306112 | tf_op jit(solution)/shard_map/dot_general | solution.py:72
  116.5 3.3 %fusion.11 = f32[256,1792]{1,0:T(8,128)} fusion(bf16[256,2048]{0,1:T(8,128)(2,1)S(1)} %collective-permute-done.3, bf16[2048,1792]{1,0:T(8,128)(2,1)S(1)} %copy-done), kind=kOutput, calls=%fused_computation.33 | convolution fusion | flops 1879048192 | bytes 10223616 | tf_op jit(solution)/shard_map/dot_general | solution.py:87
  119.9 0.5 collective-permute-start.4
  120.3 3.4 %fusion.1 = bf16[256,1,2048]{0,2,1:T(8,128)(2,1)S(1)} fusion(bf16[2048,1792]{1,0:T(8,128)(2,1)S(1)} %copy-done, bf16[256,1792]{1,0:T(8,128)(2,1)} %param.5), kind=kOutput, calls=%fused_computation.9 | convolution fusion | flops 1879572480 | bytes 9306112 | tf_op jit(solution)/shard_map/dot_general | solution.py:72
  123.9 0.5 reverse_select_fusion.2
  124.4 3.2 %copy.24 = bf16[256,2,8,2,128]{4,2,1,3,0:T(8,128)(2,1)} copy(bf16[256,2,8,2,128]{0,4,3,2,1:T(8,128)(2,1)S(1)} %bitcast.23) | data formatting | bytes 4194304 | tf_op jit(solution)/shard_map/reshape | solution.py:80
  127.6 2.8 %reverse_select_fusion.1 = bf16[256,8,2,2,128]{4,1,3,2,0:T(8,128)(2,1)S(1)} fusion(bf16[256,8,2,2,128]{4,1,3,2,0:T(8,128)(2,1)} %bitcast.24, pred[]{:T(512)S(6)} %eq.34), kind=kLoop, calls=%fused_computation.3 | loop fusion | flops 1048576 | bytes 4194305 | tf_op jit(solution)/shard_map/jit(_where)/select_n | solution.py:83
  130.4 2.0 copy.25
  132.4 5.7 %all-to-all-start = ((bf16[256,8,512]{2,0,1:T(8,128)(2,1)}), bf16[256,8,512]{2,0,1:T(8,128)(2,1)S(1)}, u32[]{:S(2)}, u32[]{:S(2)}) async-start(bf16[256,8,512]{2,0,1:T(8,128)(2,1)} %copy.25), calls=%async_computation | async-start | bytes 4194304 | tf_op jit(solution)/shard_map/all_to_all | solution.py:86
  138.1 58.9 %reduce-scatter.2.cloned.1.call-done = bf16[256,1792]{1,0:T(8,128)(2,1)} async-done(((bf16[2048,1792]{1,0:T(8,128)(2,1)}), bf16[256,1792]{1,0:T(8,128)(2,1)}) %reduce-scatter.2.cloned.1.call-update) | async-done | bytes 917520 | tf_op jit(solution)/shard_map/reduce_scatter | solution.py:65
  197.0 1.8 slice.19
  198.8 3.0 %collective-permute-start.5 = (bf16[128,1792]{1,0:T(8,128)(2,1)}, bf16[128,1792]{1,0:T(8,128)(2,1)}, u32[]{:S(2)}, u32[]{:S(2)}) collective-permute-start(bf16[128,1792]{1,0:T(8,128)(2,1)} %slice.19), channel_id=1, source_target_pairs={{0,16},{16,0},{1,17},{17,1},{2,18},{18,2},{3,19},{19,3},{4,20},{20... | collective-permute-start | bytes 1376264 | tf_op jit(solution)/shard_map/ppermute | solution.py:68
  201.8 6.6 %fusion = bf16[256,1792]{1,0:T(8,128)(2,1)} fusion(f32[256,1792]{1,0:T(8,128)} %collective-permute-done.4, bf16[256,2048]{0,1:T(8,128)(2,1)S(1)} %bitcast.27, bf16[2048,1792]{1,0:T(8,128)(2,1)} %all-gather.3.cloned.1.call-done), kind=kOutput, calls=%fused_computation.8 | convolution fusion | flops 1879965696 | bytes 11141120 | tf_op jit(solution)/shard_map/dot_general | solution.py:89
  208.4 1.0 reduce_sum.30
  209.5 3.3 %collective-permute-done.5 = bf16[128,1792]{1,0:T(8,128)(2,1)} collective-permute-done((bf16[128,1792]{1,0:T(8,128)(2,1)}, bf16[128,1792]{1,0:T(8,128)(2,1)}, u32[]{:S(2)}, u32[]{:S(2)}) %collective-permute-start.5) | collective-permute-done | bytes 458784 | tf_op jit(solution)/shard_map/ppermute | solution.py:68
  212.8 1.9 add_convert_fusion
  (37 shorter events, 1.7 us)
Async XLA Ops:
  7.2 16.2 %copy-start.5 = (u32[256]{0:T(256)S(1)}, u32[256]{0:T(256)}, u32[]{:S(2)}) copy-start(u32[256]{0:T(256)} %constant.44) | copy-start | bytes 3076
  7.2 17.5 %copy-start.4 = (s32[4]{0:T(128)S(1)}, s32[4]{0:T(128)}, u32[]{:S(2)}) copy-start(s32[4]{0:T(128)} %param.8) | copy-start | bytes 52
  7.2 17.5 %copy-start.3 = (s32[4]{0:T(128)S(1)}, s32[4]{0:T(128)}, u32[]{:S(2)}) copy-start(s32[4]{0:T(128)} %param.9) | copy-start | bytes 52
  7.2 40.0 %copy-start.1 = (bf16[256,4096]{1,0:T(8,128)(2,1)S(1)}, bf16[256,4096]{1,0:T(8,128)(2,1)}, u32[]{:S(2)}) copy-start(bf16[256,4096]{1,0:T(8,128)(2,1)} %param.7) | copy-start | bytes 6291460
  7.2 103.7 %all-gather.3.cloned.1.call-start = ((), (), s32[]{:S(2)}) async-start(), calls=%async_computation.2 | async-start | bytes 8257536 | tf_op jit(solution)/shard_map/all_gather | solution.py:54
  7.3 14.1 %collective-permute-start = (bf16[128,1792]{1,0:T(8,128)(2,1)}, bf16[128,1792]{1,0:T(8,128)(2,1)S(1)}, u32[]{:S(2)}, u32[]{:S(2)}) collective-permute-start(bf16[128,1792]{1,0:T(8,128)(2,1)} %param.6), channel_id=1, source_target_pairs={{0,16},{16,0},{1,17},{17,1},{2,18},{18,2},{3,19},{19,3},{4,20},{20... | collective-permute-start | bytes 1376264 | tf_op jit(solution)/shard_map/ppermute | solution.py:53
  23.3 173.7 %reduce-scatter.2.cloned.1.call-start = ((), (), s32[]{:S(2)}) async-start(), calls=%async_computation.3 | async-start | bytes 8257536 | tf_op jit(solution)/shard_map/reduce_scatter | solution.py:65
  59.7 4.3 %collective-permute-start.3 = (bf16[256,2048]{0,1:T(8,128)(2,1)}, bf16[256,2048]{0,1:T(8,128)(2,1)S(1)}, u32[]{:S(2)}, u32[]{:S(2)}) collective-permute-start(bf16[256,2048]{0,1:T(8,128)(2,1)} %bitcast.10), channel_id=1, source_target_pairs={{0,8},{8,0},{1,9},{9,1},{2,10},{10,2},{3,11},{11,3},{4,12},{12,4},... | collective-permute-start | bytes 3145736 | tf_op jit(solution)/shard_map/ppermute | solution.py:51
  59.7 4.3 %collective-permute-start.1 = (bf16[256,1792]{1,0:T(8,128)(2,1)}, bf16[256,1792]{1,0:T(8,128)(2,1)}, u32[]{:S(2)}, u32[]{:S(2)}) collective-permute-start(bf16[256,1792]{1,0:T(8,128)(2,1)} %param.5), channel_id=1, source_target_pairs={{0,8},{8,0},{1,9},{9,1},{2,10},{10,2},{3,11},{11,3},{4,12},{12,4},... | collective-permute-start | bytes 2752520 | tf_op jit(solution)/shard_map/ppermute | solution.py:52
  110.9 5.6 %copy-start = (bf16[2048,1792]{1,0:T(8,128)(2,1)S(1)}, bf16[2048,1792]{1,0:T(8,128)(2,1)}, u32[]{:S(2)}) copy-start(bf16[2048,1792]{1,0:T(8,128)(2,1)} %all-gather.3.cloned.1.call-done) | copy-start | bytes 22020100
  116.4 7.3 %collective-permute-start.2 = (bf16[256,2048]{0,1:T(8,128)(2,1)S(1)}, bf16[256,2048]{0,1:T(8,128)(2,1)S(1)}, u32[]{:S(2)}, u32[]{:S(2)}) collective-permute-start(bf16[256,2048]{0,1:T(8,128)(2,1)S(1)} %fusion.2), channel_id=1, source_target_pairs={{0,8},{8,0},{1,9},{9,1},{2,10},{10,2},{3,11},{11,3},{4,12},{12,4},... | collective-permute-start | bytes 3145736 | tf_op jit(solution)/shard_map/ppermute | solution.py:77
  119.9 82.0 %collective-permute-start.4 = (f32[256,1792]{1,0:T(8,128)}, f32[256,1792]{1,0:T(8,128)}, u32[]{:S(2)}, u32[]{:S(2)}) collective-permute-start(f32[256,1792]{1,0:T(8,128)} %fusion.11), channel_id=1, source_target_pairs={{0,8},{8,0},{1,9},{9,1},{2,10},{10,2},{3,11},{11,3},{4,12},{12,4},... | collective-permute-start | bytes 5505032 | tf_op jit(solution)/shard_map/ppermute | solution.py:90
  132.4 76.1 %all-to-all-start = ((bf16[256,8,512]{2,0,1:T(8,128)(2,1)}), bf16[256,8,512]{2,0,1:T(8,128)(2,1)S(1)}, u32[]{:S(2)}, u32[]{:S(2)}) async-start(bf16[256,8,512]{2,0,1:T(8,128)(2,1)} %copy.25), calls=%async_computation | async-start | bytes 4194304 | tf_op jit(solution)/shard_map/all_to_all | solution.py:86
  198.8 14.0 %collective-permute-start.5 = (bf16[128,1792]{1,0:T(8,128)(2,1)}, bf16[128,1792]{1,0:T(8,128)(2,1)}, u32[]{:S(2)}, u32[]{:S(2)}) collective-permute-start(bf16[128,1792]{1,0:T(8,128)(2,1)} %slice.19), channel_id=1, source_target_pairs={{0,16},{16,0},{1,17},{17,1},{2,18},{18,2},{3,19},{19,3},{4,20},{20... | collective-permute-start | bytes 1376264 | tf_op jit(solution)/shard_map/ppermute | solution.py:68
  208.4 4.4 %copy-start.2 = (bf16[256,1792]{1,0:T(8,128)(2,1)S(1)}, bf16[256,1792]{1,0:T(8,128)(2,1)}, u32[]{:S(2)}) copy-start(bf16[256,1792]{1,0:T(8,128)(2,1)} %reduce-scatter.2.cloned.1.call-done) | copy-start | bytes 2752516
Sparse Core Ops, SparseCore 0:
  23.5 87.3 all-gather.2
  113.4 83.5 reduce-scatter.1
where the time goes:
time: 222 us
  waiting for transfers between devices  115 us (52%)
  matrix products  26.4 us (12%)
  blocking collectives  21.3 us (10%)
  local copies, waits for them, and re-layouts  16.6 us (7%)
  between operations  14.9 us (7%)
  other arithmetic  13.9 us (6%)
  starting transfers between devices  13.2 us (6%)
    reduce_scatter x1, waiting for transfers between devices, shards(): lax.psum_scatter(grad_part, 'z', scatter_dimension=0, tiled=True)  58.9 us
    all_gather x1, waiting for transfers between devices, shards(): gathered = lax.all_gather(gathered, 'z', axis=0, tiled=True)  39.2 us
    unnamed x1, blocking collectives  21.3 us
    ppermute x1, waiting for transfers between devices, shards(): lax.ppermute(down_weight, 'yhi', swap)  10.8 us
    dot_general x2, matrix products, value_of(): lax.dot_general(rows, gathered, (((1,), (1,)), ((), ())), preferred_eleme...  8.89 us
    dot_general x1, matrix products, shards(): lax.dot_general(jnp.concatenate([weighted_mine, weighted_recv], axis=0),...  7.53 us
    dot_general x1, matrix products, shards(): jnp.dot(weighted_mine, gathered, preferred_element_type=jnp.float32)  6.61 us
    all_to_all x1, starting transfers between devices, shards(): lax.all_to_all(partial_value, 'tensor', 1, 1, tiled=True)  5.7 us
  transfers between devices with their start and end apart: 9, of which 5 were waited for; matrix products, arithmetic and copies ran while one was open for 24% of the time, Pallas kernels for 0%

commit v1 on v0

--- a/solution.py
+++ b/solution.py
@@ -51,7 +51,16 @@
     weighted_recv = lax.ppermute(weighted_theirs.reshape(tokens_here, d_half), "core", swap)
     hidden_recv = lax.ppermute(hidden, "core", swap)
     gathered = jnp.concatenate([down_weight, lax.ppermute(down_weight, "yhi", swap)], axis=0)
-    gathered = lax.all_gather(gathered, "z", axis=0, tiled=True)
+
+    def map_detail(frame_in):
+        return jnp.concatenate(
+            lax.all_to_all(
+                jnp.stack(tuple((frame_in for _ in range(lax.axis_size("z")))), axis=0), "z", 0, 0
+            ),
+            axis=0,
+        )
+
+    gathered = map_detail(gathered)
     scale = 1.0 / math.sqrt(tokens_here * n_sample)
     grad_part = (
         lax.dot_general(

time: 222 us -> 348 us (1.57)
  waiting for transfers between devices: 115 us -> 228 us
  starting transfers between devices: 13.2 us -> 18.5 us
  local copies, waits for them, and re-layouts: 16.6 us -> 21.9 us
  matrix products: 26.4 us -> 31.4 us
  other arithmetic: 13.9 us -> 10.1 us
    all_to_all x0 -> x1, waiting for transfers between devices: none -> 202 us  [map_detail(): lax.all_to_all(jnp.stack(tuple((frame_in for _ in range(lax.axis_size('z'...]
    reduce_scatter x1, waiting for transfers between devices: 58.9 us -> 0.01 us  [shards(): lax.psum_scatter(grad_part, 'z', scatter_dimension=0, tiled=True)]
    all_gather x1 -> x0, waiting for transfers between devices: 39.2 us -> none  [shards(): gathered = lax.all_gather(gathered, 'z', axis=0, tiled=True)]
    all_to_all x1, waiting for transfers between devices: 0.01 us -> 15.5 us  [shards(): lax.all_to_all(partial_value, 'tensor', 1, 1, tiled=True)]
    ppermute x1, waiting for transfers between devices: 10.8 us -> 0.01 us  [shards(): lax.ppermute(down_weight, 'yhi', swap)]
    all_to_all x0 -> x1, starting transfers between devices: none -> 4.85 us  [map_detail(): lax.all_to_all(jnp.stack(tuple((frame_in for _ in range(lax.axis_size('z'...]
    ppermute x1, waiting for transfers between devices: 3.33 us -> 7.98 us  [shards(): lax.ppermute(grad_part[rows_w:], 'yhi', swap).astype(jnp.float32)]
    another operation x0 -> x1, local copies, waits for them, and re-layouts: none -> 3.51 us  [map_detail(): jnp.stack(tuple((frame_in for _ in range(lax.axis_size('z')))), axis=0)]
  transfers between devices with their start and end apart: 9 -> 9, of which waited for: 5 -> 4; matrix products, arithmetic and copies ran while one was open for 24% -> 17% of each run, Pallas kernels for 0% -> 0%
where the time goes in v1:
time: 348 us
  waiting for transfers between devices  228 us (66%)
  matrix products  31.4 us (9%)
  blocking collectives  22.6 us (6%)
  local copies, waits for them, and re-layouts  21.9 us (6%)
  starting transfers between devices  18.5 us (5%)
  between operations  14.8 us (4%)
  other arithmetic  10.1 us (3%)
    all_to_all x1, waiting for transfers between devices, map_detail(): lax.all_to_all(jnp.stack(tuple((frame_in for _ in range(lax.axis_size('z'...  202 us
    unnamed x1, blocking collectives  22.6 us
    all_to_all x1, waiting for transfers between devices, shards(): lax.all_to_all(partial_value, 'tensor', 1, 1, tiled=True)  15.5 us
    dot_general x2, matrix products, value_of(): lax.dot_general(rows, gathered, (((1,), (1,)), ((), ())), preferred_eleme...  10.8 us
    ppermute x1, waiting for transfers between devices, shards(): lax.ppermute(grad_part[rows_w:], 'yhi', swap).astype(jnp.float32)  7.98 us
    dot_general x1, matrix products, shards(): lax.dot_general(jnp.concatenate([weighted_mine, weighted_recv], axis=0),...  7.46 us
  transfers between devices with their start and end apart: 9, of which 4 were waited for; matrix products, arithmetic and copies ran while one was open for 17% of the time, Pallas kernels for 0%

profile of v1, /device:TPU:2, one launch (start us, length us, event | category | flops | bytes accessed | tf_op | source)
XLA Modules:
  0.0 347.7 jit_solution(126594929527683922)
XLA Ops:
  7.2 3.3 collective-permute-start
  10.4 1.3 dynamic-slice
  12.4 0.8 add_dynamic-update-slice_fusion
  13.2 22.6 %all-reduce = s32[256]{0:T(256)S(1)} all-reduce(s32[256]{0:T(256)S(1)} %add_dynamic-update-slice_fusion), channel_id=2, replica_groups=mesh['z'=8,'yhi'=2,'core'=2,'tensor'=8] {'z','yhi','core'}, use_global_device_ids=true, to_apply=%add | all-reduce | flops 256 | bytes 2048
  36.0 3.3 copy.26
  40.3 3.5 %stack.8 = bf16[8,256,1792]{2,1,0:T(8,128)(2,1)} broadcast(bf16[256,1792]{1,0:T(8,128)(2,1)S(1)} %pad_maximum_fusion.1), dimensions={1,2} | broadcast | bytes 8257536 | tf_op jit(solution)/shard_map/stack | solution.py:58
  43.8 4.8 %all-to-all-start = ((bf16[8,256,1792]{2,1,0:T(8,128)(2,1)}), bf16[8,256,1792]{2,1,0:T(8,128)(2,1)}, u32[]{:S(2)}, u32[]{:S(2)}) async-start(bf16[8,256,1792]{2,1,0:T(8,128)(2,1)} %stack.8), calls=%async_computation | async-start | bytes 14680064 | tf_op jit(solution)/shard_map/all_to_all | solution.py:57
  48.7 1.8 multiply_convert_fusion.1
  50.5 3.5 copy.28
  54.0 0.5 reverse_select_fusion
  54.9 1.6 copy.30
  56.5 0.5 collective-permute-start.1
  57.0 0.8 copy.29
  57.8 3.0 collective-permute-done.1
  60.8 7.5 %multiply_convert_fusion = bf16[2048,1792]{1,0:T(8,128)(2,1)} fusion(bf16[256,2048]{0,1:T(8,128)(2,1)S(1)} %collective-permute-done.3, bf16[256,2048]{0,1:T(8,128)(2,1)S(1)} %bitcast.27, bf16[256,1792]{1,0:T(8,128)(2,1)} %collective-permute-done.1, bf16[256,1792]{1,0:T(8,128)(2,1)} %param.5), kind=kOutput, calls=%fused_computation | convolution fusion | flops 3773300736 | bytes 11272192 | tf_op jit(solution)/shard_map/dot_general | solution.py:66
  68.3 201.8 %all-to-all-done = bf16[8,256,1792]{2,1,0:T(8,128)(2,1)} async-done(((bf16[8,256,1792]{2,1,0:T(8,128)(2,1)}), bf16[8,256,1792]{2,1,0:T(8,128)(2,1)}, u32[]{:S(2)}, u32[]{:S(2)}) %all-to-all-start) | async-done | bytes 7340064 | tf_op jit(solution)/shard_map/all_to_all | solution.py:57
  270.1 5.5 %fusion.1 = bf16[256,2048]{0,1:T(8,128)(2,1)S(1)} fusion(bf16[2048,1792]{1,0:T(8,128)(2,1)} %bitcast, bf16[256,1792]{1,0:T(8,128)(2,1)} %collective-permute-done.1), kind=kOutput, calls=%fused_computation.8 | convolution fusion | flops 1879572480 | bytes 9306112 | tf_op jit(solution)/shard_map/dot_general | solution.py:81
  275.8 6.5 %fusion.10 = f32[256,1792]{1,0:T(8,128)} fusion(bf16[256,2048]{0,1:T(8,128)(2,1)S(1)} %collective-permute-done.3, bf16[2048,1792]{1,0:T(8,128)(2,1)} %bitcast), kind=kOutput, calls=%fused_computation.32 | convolution fusion | flops 1879048192 | bytes 10223616 | tf_op jit(solution)/shard_map/dot_general | solution.py:96
  282.4 0.4 collective-permute-start.4
  282.8 5.4 %fusion = bf16[256,1,2048]{0,2,1:T(8,128)(2,1)S(1)} fusion(bf16[2048,1792]{1,0:T(8,128)(2,1)} %bitcast, bf16[256,1792]{1,0:T(8,128)(2,1)} %param.5), kind=kOutput, calls=%fused_computation.7 | convolution fusion | flops 1879572480 | bytes 9306112 | tf_op jit(solution)/shard_map/dot_general | solution.py:81
  288.4 0.5 reverse_select_fusion.2
  288.9 3.2 copy.24
  292.1 2.8 reverse_select_fusion.1
  294.8 2.1 copy.25
  296.9 6.0 %all-to-all-start.1 = ((bf16[256,8,512]{2,0,1:T(8,128)(2,1)}), bf16[256,8,512]{2,0,1:T(8,128)(2,1)S(1)}, u32[]{:S(2)}, u32[]{:S(2)}) async-start(bf16[256,8,512]{2,0,1:T(8,128)(2,1)} %copy.25), calls=%async_computation.1 | async-start | bytes 4194304 | tf_op jit(solution)/shard_map/all_to_all | solution.py:95
  302.9 1.8 slice.19
  304.7 3.2 collective-permute-start.5
  307.9 6.6 %add_convert_fusion = bf16[256,1792]{1,0:T(8,128)(2,1)} fusion(f32[256,1792]{1,0:T(8,128)} %collective-permute-done.4, bf16[256,2048]{0,1:T(8,128)(2,1)S(1)} %bitcast.28, bf16[2048,1792]{1,0:T(8,128)(2,1)} %bitcast), kind=kOutput, calls=%fused_computation.16 | convolution fusion | flops 1879965696 | bytes 11141120 | tf_op jit(solution)/shard_map/dot_general | solution.py:98
  314.5 15.5 %all-to-all-done.1 = bf16[256,8,512]{2,0,1:T(8,128)(2,1)S(1)} async-done(((bf16[256,8,512]{2,0,1:T(8,128)(2,1)}), bf16[256,8,512]{2,0,1:T(8,128)(2,1)S(1)}, u32[]{:S(2)}, u32[]{:S(2)}) %all-to-all-start.1) | async-done | bytes 2097184 | tf_op jit(solution)/shard_map/all_to_all | solution.py:95
  330.0 1.0 reduce_sum.30
  331.0 8.0 %collective-permute-done.5 = bf16[128,1792]{1,0:T(8,128)(2,1)} collective-permute-done((bf16[128,1792]{1,0:T(8,128)(2,1)}, bf16[128,1792]{1,0:T(8,128)(2,1)}, u32[]{:S(2)}, u32[]{:S(2)}) %collective-permute-start.5) | collective-permute-done | bytes 458784 | tf_op jit(solution)/shard_map/ppermute | solution.py:77
  339.0 1.9 add_convert_fusion.1
  (33 shorter events, 2.0 us)
Async XLA Ops:
  7.2 33.1 %collective-permute-start = (bf16[128,1792]{1,0:T(8,128)(2,1)}, bf16[128,1792]{1,0:T(8,128)(2,1)S(1)}, u32[]{:S(2)}, u32[]{:S(2)}) collective-permute-start(bf16[128,1792]{1,0:T(8,128)(2,1)} %param.6), channel_id=1, source_target_pairs={{0,16},{16,0},{1,17},{17,1},{2,18},{18,2},{3,19},{19,3},{4,20},{20... | collective-permute-start | bytes 1376264 | tf_op jit(solution)/shard_map/ppermute | solution.py:53
  36.0 3.9 %copy-start.2 = (s32[4]{0:T(128)S(1)}, s32[4]{0:T(128)}, u32[]{:S(2)}) copy-start(s32[4]{0:T(128)} %param.9) | copy-start | bytes 52
  36.0 4.1 %copy-start.3 = (s32[4]{0:T(128)S(1)}, s32[4]{0:T(128)}, u32[]{:S(2)}) copy-start(s32[4]{0:T(128)} %param.8) | copy-start | bytes 52
  36.0 4.3 %copy-start.1 = (bf16[128,1792]{1,0:T(8,128)(2,1)S(1)}, bf16[128,1792]{1,0:T(8,128)(2,1)}, u32[]{:S(2)}) copy-start(bf16[128,1792]{1,0:T(8,128)(2,1)} %param.6) | copy-start | bytes 1376260
  43.8 226.3 %all-to-all-start = ((bf16[8,256,1792]{2,1,0:T(8,128)(2,1)}), bf16[8,256,1792]{2,1,0:T(8,128)(2,1)}, u32[]{:S(2)}, u32[]{:S(2)}) async-start(bf16[8,256,1792]{2,1,0:T(8,128)(2,1)} %stack.8), calls=%async_computation | async-start | bytes 14680064 | tf_op jit(solution)/shard_map/all_to_all | solution.py:57
  48.7 254.2 %reduce-scatter.2.cloned.1.call-start = ((), (), s32[]{:S(2)}) async-start(), calls=%async_computation.3 | async-start | bytes 8257536 | tf_op jit(solution)/shard_map/reduce_scatter | solution.py:74
  56.5 4.3 %collective-permute-start.3 = (bf16[256,2048]{0,1:T(8,128)(2,1)}, bf16[256,2048]{0,1:T(8,128)(2,1)S(1)}, u32[]{:S(2)}, u32[]{:S(2)}) collective-permute-start(bf16[256,2048]{0,1:T(8,128)(2,1)} %bitcast.11), channel_id=1, source_target_pairs={{0,8},{8,0},{1,9},{9,1},{2,10},{10,2},{3,11},{11,3},{4,12},{12,4},... | collective-permute-start | bytes 3145736 | tf_op jit(solution)/shard_map/ppermute | solution.py:51
  56.5 4.3 %collective-permute-start.1 = (bf16[256,1792]{1,0:T(8,128)(2,1)}, bf16[256,1792]{1,0:T(8,128)(2,1)}, u32[]{:S(2)}, u32[]{:S(2)}) collective-permute-start(bf16[256,1792]{1,0:T(8,128)(2,1)} %param.5), channel_id=1, source_target_pairs={{0,8},{8,0},{1,9},{9,1},{2,10},{10,2},{3,11},{11,3},{4,12},{12,4},... | collective-permute-start | bytes 2752520 | tf_op jit(solution)/shard_map/ppermute | solution.py:52
  275.5 12.6 %collective-permute-start.2 = (bf16[256,2048]{0,1:T(8,128)(2,1)S(1)}, bf16[256,2048]{0,1:T(8,128)(2,1)S(1)}, u32[]{:S(2)}, u32[]{:S(2)}) collective-permute-start(bf16[256,2048]{0,1:T(8,128)(2,1)S(1)} %fusion.1), channel_id=1, source_target_pairs={{0,8},{8,0},{1,9},{9,1},{2,10},{10,2},{3,11},{11,3},{4,12},{12,4},... | collective-permute-start | bytes 3145736 | tf_op jit(solution)/shard_map/ppermute | solution.py:86
  282.4 25.5 %collective-permute-start.4 = (f32[256,1792]{1,0:T(8,128)}, f32[256,1792]{1,0:T(8,128)}, u32[]{:S(2)}, u32[]{:S(2)}) collective-permute-start(f32[256,1792]{1,0:T(8,128)} %fusion.10), channel_id=1, source_target_pairs={{0,8},{8,0},{1,9},{9,1},{2,10},{10,2},{3,11},{11,3},{4,12},{12,4},... | collective-permute-start | bytes 5505032 | tf_op jit(solution)/shard_map/ppermute | solution.py:99
  296.9 33.1 %all-to-all-start.1 = ((bf16[256,8,512]{2,0,1:T(8,128)(2,1)}), bf16[256,8,512]{2,0,1:T(8,128)(2,1)S(1)}, u32[]{:S(2)}, u32[]{:S(2)}) async-start(bf16[256,8,512]{2,0,1:T(8,128)(2,1)} %copy.25), calls=%async_computation.1 | async-start | bytes 4194304 | tf_op jit(solution)/shard_map/all_to_all | solution.py:95
  304.7 34.3 %collective-permute-start.5 = (bf16[128,1792]{1,0:T(8,128)(2,1)}, bf16[128,1792]{1,0:T(8,128)(2,1)}, u32[]{:S(2)}, u32[]{:S(2)}) collective-permute-start(bf16[128,1792]{1,0:T(8,128)(2,1)} %slice.19), channel_id=1, source_target_pairs={{0,16},{16,0},{1,17},{17,1},{2,18},{18,2},{3,19},{19,3},{4,20},{20... | collective-permute-start | bytes 1376264 | tf_op jit(solution)/shard_map/ppermute | solution.py:77
  314.5 24.5 %copy-start = (bf16[256,1792]{1,0:T(8,128)(2,1)S(1)}, bf16[256,1792]{1,0:T(8,128)(2,1)}, u32[]{:S(2)}) copy-start(bf16[256,1792]{1,0:T(8,128)(2,1)} %reduce-scatter.2.cloned.1.call-done) | copy-start | bytes 2752516
Sparse Core Ops, SparseCore 0:
  68.4 208.1 reduce-scatter.1
